TPU v7x, 256 devices: a whole 4x4x8 slice. The times are simulated.
256 devices in a mesh: seq: 32 (over z, y_hi, core), tp: 8 (over y_lo, x).
Axes of the slice: x: 4, y: 4 (y_hi: 2, y_lo: 2; y = y_hi * 2 + y_lo), z: 8, core: 2. Of those that a mesh axis runs over, the one named last changes fastest.
Arguments:
- queries: bfloat16 [12288, 3072], P('seq', 'tp'), may hold values from -16 to 16
- keys: bfloat16 [12288, 3072], P('seq', 'tp'), may hold values from -6 to 6
- values: bfloat16 [12288, 3072], P('seq', 'tp'), may hold values from -6 to 6
- resid: bfloat16 [12288, 6144], P(('seq', 'tp')), may hold values from -6 to 6
- out_weight: bfloat16 [3072, 6144], P('tp'), may hold values from -0.109375 to 0.109375
- gain: float32 [6144], replicated, may hold values from 0.1 to 1.9
- pair_of_device: int32 [32], replicated, may hold values from 0 to 31, each once
- frame_of_tile: int32 [64], replicated, may hold values from 0 to 8, as said below
Outputs:
- layer_out: bfloat16 [12288, 6144], P(('seq', 'tp'))
Inputs may be any that keep to these rules, and one draw needn't show every extreme that they name: `pair_of_device`: each value once. Frames have equal length, 8 tiles; the sequence starts inside frame 0 and ends inside frame 8, so only these two are partial: frame_of_tile[t] = (t + o) // 8 for an offset o from 1 to 7.
All inputs are finite; a program needn't handle non-finite values.
Results may differ from a plain program's by a relative error of at most 0.025.
Values may be sent and summed in bfloat16 or wider, within the bound.
No kernel may reach another device: no remote copies, remote signals or barrier semaphores. Data moves between devices by JAX's collectives and lax.ppermute only.
A program may use at most 128 MiB of HBM per device.

v0:
```python
import math
import jax
import jax.numpy as jnp
from jax import lax
from jax.sharding import PartitionSpec as P

HEAD = 128


def slot_frames(pair_of_device, frame_of_tile, tile_count):
    slot_ids = jnp.arange(tile_count, dtype=jnp.int32)
    paired = jnp.repeat(pair_of_device, 2)
    tile_ids = jnp.where(slot_ids % 2 == 0, paired, tile_count - 1 - paired)
    matches = tile_ids[:, None] == jnp.arange(tile_count, dtype=jnp.int32)[None, :]
    return jnp.sum(jnp.where(matches, frame_of_tile[None, :], 0), axis=1)


def frames_of_rows(slot_frame, offset, row_count, span_rows):
    row_slots = (offset + jnp.arange(row_count, dtype=jnp.int32)) // span_rows
    matches = row_slots[:, None] == jnp.arange(slot_frame.shape[0], dtype=jnp.int32)[None, :]
    return jnp.sum(jnp.where(matches, slot_frame[None, :], 0), axis=1)


def softmax_update(carry_state, query_heads, query_frame, key_rows, value_rows, key_frame):
    head_count = query_heads.shape[1]
    key_heads = key_rows.reshape(key_rows.shape[0], head_count, HEAD)
    value_heads = value_rows.reshape(value_rows.shape[0], head_count, HEAD)
    allowed = (key_frame[None, :] <= query_frame[:, None])[None, :, :]
    score_scale = 1.0 / math.sqrt(HEAD)
    run_max, run_totals, weighted = carry_state
    scores = (
        jnp.einsum("qhd,khd->hqk", query_heads, key_heads, preferred_element_type=jnp.float32)
        * score_scale
    )
    masked = jnp.where(allowed, scores, jnp.float32(-1e30))
    new_max = jnp.maximum(run_max, jnp.max(masked, axis=-1))
    probs = jnp.where(allowed, jnp.exp(masked - new_max[..., None]), jnp.float32(0.0))
    rescale = jnp.exp(run_max - new_max)
    new_totals = run_totals * rescale + jnp.sum(probs, axis=-1)
    product = jnp.einsum(
        "hqk,khd->hqd", probs.astype(jnp.bfloat16), value_heads, preferred_element_type=jnp.float32
    )
    return (new_max, new_totals, weighted * rescale[..., None] + product)


def empty_state(head_count, row_count):
    return (
        jnp.full((head_count, row_count), -1e30, jnp.float32),
        jnp.zeros((head_count, row_count), jnp.float32),
        jnp.zeros((head_count, row_count, HEAD), jnp.float32),
    )


def local(queries, keys, values, resid, out_weight, gain, pair_of_device, frame_of_tile):
    tok_rows, row_width = queries.shape
    head_count = row_width // HEAD
    span_rows = tok_rows // 2
    seq_count = lax.axis_size("seq")
    seq_index = lax.axis_index("seq")
    slot_frame = slot_frames(pair_of_device, frame_of_tile, 2 * seq_count)
    own_frames = lax.dynamic_slice_in_dim(slot_frame, 2 * seq_index, 2, 0)
    row_frame = jnp.repeat(own_frames, span_rows)
    query_heads = queries.reshape(tok_rows, head_count, HEAD)
    key_rows = lax.all_gather(keys, "seq", axis=0, tiled=True)
    value_rows = lax.all_gather(values, "seq", axis=0, tiled=True)
    key_count = key_rows.shape[0]
    key_blocks = key_rows.reshape(key_count // 512, 512, row_width)
    value_blocks = value_rows.reshape(key_count // 512, 512, row_width)

    def advance(inner_state, entry):
        key_block, value_block, block_index = entry
        key_frame = frames_of_rows(slot_frame, block_index * 512, 512, span_rows)
        return (
            softmax_update(inner_state, query_heads, row_frame, key_block, value_block, key_frame),
            None,
        )

    final_state, unused = lax.scan(
        advance,
        empty_state(head_count, tok_rows),
        (key_blocks, value_blocks, jnp.arange(key_count // 512, dtype=jnp.int32)),
    )
    run_max, run_totals, weighted = final_state
    attn_heads = jnp.transpose(weighted / run_totals[..., None], (1, 0, 2))
    attn = attn_heads.reshape(tok_rows, row_width).astype(jnp.bfloat16)
    branch = lax.psum_scatter(
        jnp.dot(attn, out_weight, preferred_element_type=jnp.float32).astype(jnp.bfloat16),
        "tp",
        scatter_dimension=0,
        tiled=True,
    ).astype(jnp.float32)
    rms = jnp.sqrt(jnp.mean(branch * branch, axis=-1) + 1e-06)
    layer_out = resid.astype(jnp.float32) + gain[None, :] * branch / rms[:, None]
    return layer_out.astype(jnp.bfloat16)


def solution(mesh):
    in_specs = (
        P("seq", "tp"),
        P("seq", "tp"),
        P("seq", "tp"),
        P(("seq", "tp"), None),
        P("tp", None),
        P(),
        P(),
        P(),
    )
    out_specs = P(("seq", "tp"), None)
    return jax.shard_map(local, mesh=mesh, in_specs=in_specs, out_specs=out_specs, check_vma=False)
```

profile of v0, /device:TPU:1, one launch (start us, length us, event | category | flops | bytes accessed | tf_op | source)
XLA Modules:
  0.0 436.5 jit_solution(12909804964037090042)
XLA Ops:
  8.9 1.2 copy.27
  11.2 108.5 %all-gather.3.cloned.1.call-done = bf16[12288,384]{1,0:T(8,128)(2,1)} async-done(((bf16[384,384]{1,0:T(8,128)(2,1)}), bf16[12288,384]{1,0:T(8,128)(2,1)}) %all-gather.3.cloned.1.call-update) | async-done | bytes 9437200 | tf_op jit(solution)/shard_map/all_gather | solution.py:64
  119.8 104.7 %all-gather.5.cloned.1.call-done = bf16[12288,384]{1,0:T(8,128)(2,1)} async-done(((bf16[384,384]{1,0:T(8,128)(2,1)}), bf16[12288,384]{1,0:T(8,128)(2,1)}) %all-gather.5.cloned.1.call-update) | async-done | bytes 9437200 | tf_op jit(solution)/shard_map/all_gather | solution.py:65
  224.5 137.8 %while.17 = (s32[]{:T(128)}, f32[3,384]{1,0:T(4,128)S(1)}, f32[3,384]{1,0:T(4,128)S(1)}, f32[3,384,128]{2,1,0:T(8,128)S(1)}, s32[24]{0:T(128)S(1)}, /*index=5*/s...) while((s32[]{:T(128)}, f32[3,384]{1,0:T(4,128)S(1)}, ...), condition=%wide.region_5.6_spmd.clone, body=%wide.region_1.5_spmd.clone.sunk | while | flops 310404736 | bytes 13359545 | solution.py:78
  226.1 1.2 constant_dynamic-slice_fusion.3
  231.9 1.2 constant_dynamic-slice_fusion.3
  237.6 1.2 constant_dynamic-slice_fusion.3
  243.4 1.2 constant_dynamic-slice_fusion.3
  249.1 1.2 constant_dynamic-slice_fusion.3
  254.9 1.2 constant_dynamic-slice_fusion.3
  260.6 1.2 constant_dynamic-slice_fusion.3
  266.3 1.2 constant_dynamic-slice_fusion.3
  272.1 1.2 constant_dynamic-slice_fusion.3
  277.8 1.2 constant_dynamic-slice_fusion.3
  283.6 1.2 constant_dynamic-slice_fusion.3
  289.3 1.2 constant_dynamic-slice_fusion.3
  295.1 1.2 constant_dynamic-slice_fusion.3
  300.8 1.2 constant_dynamic-slice_fusion.3
  306.5 1.2 constant_dynamic-slice_fusion.3
  312.3 1.2 constant_dynamic-slice_fusion.3
  318.0 1.2 constant_dynamic-slice_fusion.3
  323.8 1.2 constant_dynamic-slice_fusion.3
  329.5 1.2 constant_dynamic-slice_fusion.3
  335.3 1.2 constant_dynamic-slice_fusion.3
  341.0 1.2 constant_dynamic-slice_fusion.3
  346.7 1.2 constant_dynamic-slice_fusion.3
  352.5 1.2 constant_dynamic-slice_fusion.3
  358.2 1.2 constant_dynamic-slice_fusion.3
  362.6 7.1 %convolution_convert_fusion = bf16[384,6144]{1,0:T(8,128)(2,1)} fusion(bf16[384,384]{0,1:T(8,128)(2,1)S(1)} %bitcast.45, bf16[384,6144]{1,0:T(8,128)(2,1)} %param.14), kind=kOutput, calls=%fused_computation.29 | convolution fusion | flops 1814298624 | bytes 9732096 | tf_op jit(solution)/shard_map/dot_general | solution.py:87
  369.7 56.8 %reduce-scatter.2.cloned.1.call-done = bf16[48,6144]{1,0:T(8,128)(2,1)} async-done(((bf16[384,6144]{1,0:T(8,128)(2,1)}), bf16[48,6144]{1,0:T(8,128)(2,1)}) %reduce-scatter.2.cloned.1.call-update) | async-done | bytes 589840 | tf_op jit(solution)/shard_map/reduce_scatter | solution.py:86
  426.5 1.3 fusion.18
  427.8 2.1 fusion.17
  (359 shorter events, 96.3 us)
Async XLA Ops:
  6.5 113.2 %all-gather.3.cloned.1.call-start = ((), (), s32[]{:S(2)}) async-start(), calls=%async_computation.1 | async-start | bytes 9732096 | tf_op jit(solution)/shard_map/all_gather | solution.py:64
  7.3 217.2 %all-gather.5.cloned.1.call-start = ((), (), s32[]{:S(2)}) async-start(), calls=%async_computation.2 | async-start | bytes 9732096 | tf_op jit(solution)/shard_map/all_gather | solution.py:65
  8.0 418.5 %reduce-scatter.2.cloned.1.call-start = ((), (), s32[]{:S(2)}) async-start(), calls=%async_computation.3 | async-start | bytes 5308416 | tf_op jit(solution)/shard_map/reduce_scatter | solution.py:86
  369.7 58.1 %copy-start = (bf16[48,6144]{1,0:T(8,128)(2,1)S(1)}, bf16[48,6144]{1,0:T(8,128)(2,1)}, u32[]{:S(2)}) copy-start(bf16[48,6144]{1,0:T(8,128)(2,1)} %param.13) | copy-start | bytes 1769476
  369.7 58.1 %copy-start.1 = (f32[6144]{0:T(1024)S(1)}, f32[6144]{0:T(1024)}, u32[]{:S(2)}) copy-start(f32[6144]{0:T(1024)} %param.15) | copy-start | bytes 73732
Sparse Core Ops, SparseCore 0:
  10.1 109.5 all-gather.2
  122.5 101.8 all-gather.4
  369.8 56.6 reduce-scatter.1
where the time goes:
time: 437 us; the launch traced here: 436 us
  waiting for transfers between devices  271 us (62%)
  local copies, waits for them, and re-layouts  59.5 us (14%)
  matrix products  49.3 us (11%)
  other arithmetic  26.6 us (6%)
  loops' own time  16.4 us (4%)
  between operations  13.2 us (3%)
    all_gather x1, waiting for transfers between devices, local(): key_rows = lax.all_gather(keys, 'seq', axis=0, tiled=True)  109 us
    all_gather x1, waiting for transfers between devices, local(): value_rows = lax.all_gather(values, 'seq', axis=0, tiled=True)  105 us
    reduce_scatter x1, waiting for transfers between devices, local(): lax.psum_scatter(jnp.dot(attn, out_weight, preferred_element_type=jnp.flo...  56.8 us
    dynamic_slice x96, local copies, waits for them, and re-layouts, local(): lax.scan(advance, empty_state(head_count, tok_rows), (key_blocks, value_b...  53.2 us
    dot_general x24, matrix products, softmax_update(): jnp.einsum('hqk,khd->hqd', probs.astype(jnp.bfloat16), value_heads, prefe...  25.8 us
    another operation x1, loops' own time, local(): lax.scan(advance, empty_state(head_count, tok_rows), (key_blocks, value_b...  16.4 us
    dot_general x24, matrix products, softmax_update(): jnp.einsum('qhd,khd->hqk', query_heads, key_heads, preferred_element_type...  16.3 us
    reduce_sum x24, other arithmetic, softmax_update(): new_totals = run_totals * rescale + jnp.sum(probs, axis=-1)  14.9 us
  transfers between devices with their start and end apart: 3, of which 3 were waited for; matrix products, arithmetic and copies ran while one was open for 1% of the time, Pallas kernels for 0%

commit v1 on v0

--- a/solution.py
+++ b/solution.py
@@ -61,7 +61,10 @@
     own_frames = lax.dynamic_slice_in_dim(slot_frame, 2 * seq_index, 2, 0)
     row_frame = jnp.repeat(own_frames, span_rows)
     query_heads = queries.reshape(tok_rows, head_count, HEAD)
-    key_rows = lax.all_gather(keys, "seq", axis=0, tiled=True)
+    nodes = []
+    for _ in range(lax.axis_size("seq")):
+        nodes.append(keys)
+    key_rows = jnp.concatenate(lax.all_to_all(jnp.stack(nodes), "seq", 0, 0), axis=0)
     value_rows = lax.all_gather(values, "seq", axis=0, tiled=True)
     key_count = key_rows.shape[0]
     key_blocks = key_rows.reshape(key_count // 512, 512, row_width)

time: 437 us -> 548 us (1.25)
  matrix products: 49.3 us -> 114 us
  waiting for transfers between devices: 271 us -> 298 us
  starting transfers between devices: 0.08 us -> 13 us
  local copies, waits for them, and re-layouts: 59.5 us -> 65.2 us
    all_to_all x0 -> x1, waiting for transfers between devices: none -> 235 us  [local(): lax.all_to_all(jnp.stack(nodes), 'seq', 0, 0)]
    all_gather x1 -> x0, waiting for transfers between devices: 109 us -> none  [local(): key_rows = lax.all_gather(keys, 'seq', axis=0, tiled=True)]
    all_gather x1, waiting for transfers between devices: 105 us -> 0.01 us  [local(): value_rows = lax.all_gather(values, 'seq', axis=0, tiled=True)]
    dot_general x24, matrix products: 25.8 us -> 67.5 us  [softmax_update(): jnp.einsum('hqk,khd->hqd', probs.astype(jnp.bfloat16), value_heads, prefe...]
    dot_general x24, matrix products: 16.3 us -> 39.3 us  [softmax_update(): jnp.einsum('qhd,khd->hqk', query_heads, key_heads, preferred_element_type...]
    all_to_all x0 -> x1, starting transfers between devices: none -> 12.9 us  [local(): lax.all_to_all(jnp.stack(nodes), 'seq', 0, 0)]
    another operation x0 -> x1, local copies, waits for them, and re-layouts: none -> 6.1 us  [local(): jnp.stack(nodes)]
  transfers between devices with their start and end apart: 3 -> 3, of which waited for: 3 -> 2; matrix products, arithmetic and copies ran while one was open for 1% -> 0% of each run, Pallas kernels for 0% -> 0%
where the time goes in v1:
time: 548 us; the launch traced here: 545 us
  waiting for transfers between devices  298 us (54%)
  matrix products  114 us (21%)
  local copies, waits for them, and re-layouts  65.2 us (12%)
  other arithmetic  25.7 us (5%)
  loops' own time  16 us (3%)
  between operations  13.5 us (2%)
  starting transfers between devices  13 us (2%)
    all_to_all x1, waiting for transfers between devices, local(): lax.all_to_all(jnp.stack(nodes), 'seq', 0, 0)  235 us
    dot_general x24, matrix products, softmax_update(): jnp.einsum('hqk,khd->hqd', probs.astype(jnp.bfloat16), value_heads, prefe...  67.5 us
    reduce_scatter x1, waiting for transfers between devices, local(): lax.psum_scatter(jnp.dot(attn, out_weight, preferred_element_type=jnp.flo...  61.5 us
    dynamic_slice x96, local copies, waits for them, and re-layouts, local(): lax.scan(advance, empty_state(head_count, tok_rows), (key_blocks, value_b...  52.7 us
    dot_general x24, matrix products, softmax_update(): jnp.einsum('qhd,khd->hqk', query_heads, key_heads, preferred_element_type...  39.3 us
    another operation x1, loops' own time, local(): lax.scan(advance, empty_state(head_count, tok_rows), (key_blocks, value_b...  16 us
    reduce_sum x24, other arithmetic, softmax_update(): new_totals = run_totals * rescale + jnp.sum(probs, axis=-1)  14.7 us
    all_to_all x1, starting transfers between devices, local(): lax.all_to_all(jnp.stack(nodes), 'seq', 0, 0)  12.9 us
  transfers between devices with their start and end apart: 3, of which 2 were waited for; matrix products, arithmetic and copies ran while one was open for 0% of the time, Pallas kernels for 0%

profile of v1, /device:TPU:1, one launch (start us, length us, event | category | flops | bytes accessed | tf_op | source)
XLA Modules:
  0.0 544.9 jit_solution(14347014139067150650)
XLA Ops:
  6.5 6.1 %stack.2 = bf16[32,384,384]{2,1,0:T(8,128)(2,1)} broadcast(bf16[384,384]{1,0:T(8,128)(2,1)} %param.11), dimensions={1,2} | broadcast | bytes 9732096 | tf_op jit(solution)/shard_map/stack | solution.py:67
  12.6 12.9 %all-to-all-start = ((bf16[32,384,384]{2,1,0:T(8,128)(2,1)}), bf16[32,384,384]{2,1,0:T(8,128)(2,1)}, u32[]{:S(2)}, u32[]{:S(2)}) async-start(bf16[32,384,384]{2,1,0:T(8,128)(2,1)} %stack.2), calls=%async_computation | async-start | bytes 18874368 | tf_op jit(solution)/shard_map/all_to_all | solution.py:67
  28.0 235.4 %all-to-all-done = bf16[32,384,384]{2,1,0:T(8,128)(2,1)} async-done(((bf16[32,384,384]{2,1,0:T(8,128)(2,1)}), bf16[32,384,384]{2,1,0:T(8,128)(2,1)}, u32[]{:S(2)}, u32[]{:S(2)}) %all-to-all-start) | async-done | bytes 9437216 | tf_op jit(solution)/shard_map/all_to_all | solution.py:67
  263.4 201.3 %while.17 = (s32[]{:T(128)}, f32[3,384]{1,0:T(4,128)S(1)}, f32[3,384]{1,0:T(4,128)S(1)}, f32[3,384,128]{2,1,0:T(8,128)}, s32[24]{0:T(128)S(1)}, /*index=5*/s32[6...) while((s32[]{:T(128)}, f32[3,384]{1,0:T(4,128)S(1)}, ...), condition=%wide.region_5.6_spmd.clone, body=%wide.region_1.5_spmd.clone.sunk | while | flops 310404736 | bytes 13359537 | solution.py:81
  266.4 1.6 fusion.35
  268.9 1.8 convolution_add_fusion.2
  276.3 2.9 convolution_add_fusion.2
  284.7 2.9 convolution_add_fusion.2
  293.2 2.9 convolution_add_fusion.2
  301.6 2.9 convolution_add_fusion.2
  310.0 2.9 convolution_add_fusion.2
  318.5 2.9 convolution_add_fusion.2
  326.9 2.9 convolution_add_fusion.2
  335.3 2.9 convolution_add_fusion.2
  343.7 2.9 convolution_add_fusion.2
  352.2 2.9 convolution_add_fusion.2
  360.6 2.9 convolution_add_fusion.2
  369.0 2.9 convolution_add_fusion.2
  377.5 2.9 convolution_add_fusion.2
  385.9 2.9 convolution_add_fusion.2
  394.3 2.9 convolution_add_fusion.2
  402.7 2.9 convolution_add_fusion.2
  411.2 2.9 convolution_add_fusion.2
  419.6 2.9 convolution_add_fusion.2
  428.0 2.9 convolution_add_fusion.2
  436.5 2.9 convolution_add_fusion.2
  444.9 2.9 convolution_add_fusion.2
  453.3 2.9 convolution_add_fusion.2
  461.8 2.9 convolution_add_fusion.2
  466.0 7.1 %convolution_convert_fusion = bf16[384,6144]{1,0:T(8,128)(2,1)} fusion(bf16[384,384]{0,1:T(8,128)(2,1)S(1)} %bitcast.45, bf16[384,6144]{1,0:T(8,128)(2,1)} %param.14), kind=kOutput, calls=%fused_computation.29 | convolution fusion | flops 1814298624 | bytes 9732096 | tf_op jit(solution)/shard_map/dot_general | solution.py:90
  473.1 61.5 %reduce-scatter.2.cloned.1.call-done = bf16[48,6144]{1,0:T(8,128)(2,1)} async-done(((bf16[384,6144]{1,0:T(8,128)(2,1)}), bf16[48,6144]{1,0:T(8,128)(2,1)}) %reduce-scatter.2.cloned.1.call-update) | async-done | bytes 589840 | tf_op jit(solution)/shard_map/reduce_scatter | solution.py:89
  535.9 2.1 fusion.17
  (365 shorter events, 121.1 us)
Async XLA Ops:
  12.6 13.8 %copy-start.3 = (s32[32]{0:T(128)S(1)}, s32[32]{0:T(128)}, u32[]{:S(2)}) copy-start(s32[32]{0:T(128)} %param.16) | copy-start | bytes 388
  12.6 14.0 %copy-start.1 = (bf16[384,384]{1,0:T(8,128)(2,1)S(1)}, bf16[384,384]{1,0:T(8,128)(2,1)}, u32[]{:S(2)}) copy-start(bf16[384,384]{1,0:T(8,128)(2,1)} %param.10) | copy-start | bytes 884740
  12.6 15.1 %copy-start.4 = (s32[64]{0:T(128)S(1)}, s32[64]{0:T(128)}, u32[]{:S(2)}) copy-start(s32[64]{0:T(128)} %param.17) | copy-start | bytes 772
  12.6 250.7 %all-to-all-start = ((bf16[32,384,384]{2,1,0:T(8,128)(2,1)}), bf16[32,384,384]{2,1,0:T(8,128)(2,1)}, u32[]{:S(2)}, u32[]{:S(2)}) async-start(bf16[32,384,384]{2,1,0:T(8,128)(2,1)} %stack.2), calls=%async_computation | async-start | bytes 18874368 | tf_op jit(solution)/shard_map/all_to_all | solution.py:67
  25.6 237.8 %all-gather.2.cloned.1.call-start = ((), (), s32[]{:S(2)}) async-start(), calls=%async_computation.2 | async-start | bytes 9732096 | tf_op jit(solution)/shard_map/all_gather | solution.py:68
  26.3 508.3 %reduce-scatter.2.cloned.1.call-start = ((), (), s32[]{:S(2)}) async-start(), calls=%async_computation.3 | async-start | bytes 5308416 | tf_op jit(solution)/shard_map/reduce_scatter | solution.py:89
  473.1 62.8 %copy-start = (bf16[48,6144]{1,0:T(8,128)(2,1)S(1)}, bf16[48,6144]{1,0:T(8,128)(2,1)}, u32[]{:S(2)}) copy-start(bf16[48,6144]{1,0:T(8,128)(2,1)} %param.13) | copy-start | bytes 1769476
  473.1 62.8 %copy-start.2 = (f32[6144]{0:T(1024)S(1)}, f32[6144]{0:T(1024)}, u32[]{:S(2)}) copy-start(f32[6144]{0:T(1024)} %param.15) | copy-start | bytes 73732
Sparse Core Ops, SparseCore 0:
  29.2 181.3 all-gather.1
  473.2 61.3 reduce-scatter.1

commit v2 on v0

--- a/solution.py
+++ b/solution.py
@@ -3,8 +3,16 @@
 import jax.numpy as jnp
 from jax import lax
 from jax.sharding import PartitionSpec as P
+from jax.lax import all_gather
 
 HEAD = 128
+
+
+def unite_numbers_in(vals, arr, chip_axis):
+    front = jnp.concatenate([vals, arr], axis=1)
+    later = all_gather(front, chip_axis, axis=0, tiled=True)
+    r2 = jnp.split(later, [vals.shape[1]], axis=1)
+    return r2
 
 
 def slot_frames(pair_of_device, frame_of_tile, tile_count):
@@ -61,8 +69,7 @@
     own_frames = lax.dynamic_slice_in_dim(slot_frame, 2 * seq_index, 2, 0)
     row_frame = jnp.repeat(own_frames, span_rows)
     query_heads = queries.reshape(tok_rows, head_count, HEAD)
-    key_rows = lax.all_gather(keys, "seq", axis=0, tiled=True)
-    value_rows = lax.all_gather(values, "seq", axis=0, tiled=True)
+    key_rows, value_rows = unite_numbers_in(keys, values, "seq")
     key_count = key_rows.shape[0]
     key_blocks = key_rows.reshape(key_count // 512, 512, row_width)
     value_blocks = value_rows.reshape(key_count // 512, 512, row_width)

time: 437 us -> 461 us (1.055)
  matrix products: 49.3 us -> 114 us
  waiting for transfers between devices: 271 us -> 208 us
  local copies, waits for them, and re-layouts: 59.5 us -> 76.8 us
    all_gather x2 -> x1, waiting for transfers between devices: 213 us -> 151 us  [unite_numbers_in(): later = all_gather(front, chip_axis, axis=0, tiled=True)]
    dot_general x24, matrix products: 25.8 us -> 67.5 us  [softmax_update(): jnp.einsum('hqk,khd->hqd', probs.astype(jnp.bfloat16), value_heads, prefe...]
    dot_general x24, matrix products: 16.3 us -> 39.3 us  [softmax_update(): jnp.einsum('qhd,khd->hqk', query_heads, key_heads, preferred_element_type...]
    split x0 -> x1, local copies, waits for them, and re-layouts: none -> 14.9 us  [unite_numbers_in(): r2 = jnp.split(later, [vals.shape[1]], axis=1)]
  transfers between devices with their start and end apart: 3 -> 2, of which waited for: 3 -> 2; matrix products, arithmetic and copies ran while one was open for 1% -> 1% of each run, Pallas kernels for 0% -> 0%
where the time goes in v2:
time: 461 us; the launch traced here: 458 us
  waiting for transfers between devices  208 us (45%)
  matrix products  114 us (25%)
  local copies, waits for them, and re-layouts  76.8 us (17%)
  other arithmetic  27.6 us (6%)
  loops' own time  17.9 us (4%)
  between operations  13.5 us (3%)
    all_gather x1, waiting for transfers between devices, unite_numbers_in(): later = all_gather(front, chip_axis, axis=0, tiled=True)  151 us
    dot_general x24, matrix products, softmax_update(): jnp.einsum('hqk,khd->hqd', probs.astype(jnp.bfloat16), value_heads, prefe...  67.5 us
    reduce_scatter x1, waiting for transfers between devices, local(): lax.psum_scatter(jnp.dot(attn, out_weight, preferred_element_type=jnp.flo...  57 us
    dynamic_slice x96, local copies, waits for them, and re-layouts, local(): lax.scan(advance, empty_state(head_count, tok_rows), (key_blocks, value_b...  53.8 us
    dot_general x24, matrix products, softmax_update(): jnp.einsum('qhd,khd->hqk', query_heads, key_heads, preferred_element_type...  39.3 us
    another operation x1, loops' own time, local(): lax.scan(advance, empty_state(head_count, tok_rows), (key_blocks, value_b...  17.9 us
    split x1, local copies, waits for them, and re-layouts, unite_numbers_in(): r2 = jnp.split(later, [vals.shape[1]], axis=1)  14.9 us
    reduce_sum x24, other arithmetic, softmax_update(): new_totals = run_totals * rescale + jnp.sum(probs, axis=-1)  14.7 us
  transfers between devices with their start and end apart: 2, of which 2 were waited for; matrix products, arithmetic and copies ran while one was open for 1% of the time, Pallas kernels for 0%

profile of v2, /device:TPU:1, one launch (start us, length us, event | category | flops | bytes accessed | tf_op | source)
XLA Modules:
  0.0 457.7 jit_solution(2734207104667880823)
XLA Ops:
  6.5 1.9 pad_maximum_fusion
  11.8 150.9 %all-gather.2.cloned.1.call-done = bf16[12288,768]{1,0:T(8,128)(2,1)} async-done(((bf16[384,768]{1,0:T(8,128)(2,1)}), bf16[12288,768]{1,0:T(8,128)(2,1)}) %all-gather.2.cloned.1.call-update) | async-done | bytes 18874384 | tf_op jit(solution)/shard_map/all_gather | solution.py:13
  162.6 14.9 %fusion.19 = (bf16[12288,384]{1,0:T(8,128)(2,1)}, bf16[12288,384]{1,0:T(8,128)(2,1)}) fusion(bf16[12288,768]{1,0:T(8,128)(2,1)} %all-gather.2.cloned.1.call-done), kind=kLoop, calls=%fused_computation.43 | loop fusion | bytes 37748736 | tf_op jit(solution)/shard_map/split | solution.py:14
  177.6 204.3 %while.17 = (s32[]{:T(128)}, f32[3,384]{1,0:T(4,128)S(1)}, f32[3,384]{1,0:T(4,128)S(1)}, f32[3,384,128]{2,1,0:T(8,128)}, s32[24]{0:T(128)S(1)}, /*index=5*/s32[6...) while((s32[]{:T(128)}, f32[3,384]{1,0:T(4,128)S(1)}, ...), condition=%wide.region_5.6_spmd.clone, body=%wide.region_1.5_spmd.clone.sunk | while | flops 310404736 | bytes 13359537 | solution.py:85
  183.3 1.8 convolution_add_fusion.2
  190.8 2.9 convolution_add_fusion.2
  199.3 2.9 convolution_add_fusion.2
  205.4 1.6 fusion.36
  207.9 2.9 convolution_add_fusion.2
  216.4 2.9 convolution_add_fusion.2
  225.0 2.9 convolution_add_fusion.2
  233.6 2.9 convolution_add_fusion.2
  242.1 2.9 convolution_add_fusion.2
  250.7 2.9 convolution_add_fusion.2
  259.2 2.9 convolution_add_fusion.2
  267.8 2.9 convolution_add_fusion.2
  276.3 2.9 convolution_add_fusion.2
  284.9 2.9 convolution_add_fusion.2
  293.4 2.9 convolution_add_fusion.2
  302.0 2.9 convolution_add_fusion.2
  310.6 2.9 convolution_add_fusion.2
  319.1 2.9 convolution_add_fusion.2
  327.7 2.9 convolution_add_fusion.2
  336.2 2.9 convolution_add_fusion.2
  344.8 2.9 convolution_add_fusion.2
  353.3 2.9 convolution_add_fusion.2
  361.9 2.9 convolution_add_fusion.2
  370.4 2.9 convolution_add_fusion.2
  379.0 2.9 convolution_add_fusion.2
  383.2 7.1 %convolution_convert_fusion = bf16[384,6144]{1,0:T(8,128)(2,1)} fusion(bf16[384,384]{0,1:T(8,128)(2,1)S(1)} %bitcast.47, bf16[384,6144]{1,0:T(8,128)(2,1)} %param.14), kind=kOutput, calls=%fused_computation.29 | convolution fusion | flops 1814298624 | bytes 9732096 | tf_op jit(solution)/shard_map/dot_general | solution.py:94
  390.4 57.0 %reduce-scatter.2.cloned.1.call-done = bf16[48,6144]{1,0:T(8,128)(2,1)} async-done(((bf16[384,6144]{1,0:T(8,128)(2,1)}), bf16[48,6144]{1,0:T(8,128)(2,1)}) %reduce-scatter.2.cloned.1.call-update) | async-done | bytes 589840 | tf_op jit(solution)/shard_map/reduce_scatter | solution.py:93
  448.7 2.1 fusion.17
  (360 shorter events, 123.2 us)
Async XLA Ops:
  6.5 5.0 %copy-start.2 = (s32[64]{0:T(128)S(1)}, s32[64]{0:T(128)}, u32[]{:S(2)}) copy-start(s32[64]{0:T(128)} %param.17) | copy-start | bytes 772
  6.5 156.1 %all-gather.2.cloned.1.call-start = ((), (), s32[]{:S(2)}) async-start(), calls=%async_computation.1 | async-start | bytes 19464192 | tf_op jit(solution)/shard_map/all_gather | solution.py:13
  8.5 438.9 %reduce-scatter.2.cloned.1.call-start = ((), (), s32[]{:S(2)}) async-start(), calls=%async_computation.2 | async-start | bytes 5308416 | tf_op jit(solution)/shard_map/reduce_scatter | solution.py:93
  390.3 58.4 %copy-start = (bf16[48,6144]{1,0:T(8,128)(2,1)S(1)}, bf16[48,6144]{1,0:T(8,128)(2,1)}, u32[]{:S(2)}) copy-start(bf16[48,6144]{1,0:T(8,128)(2,1)} %param.13) | copy-start | bytes 1769476
  390.3 58.4 %copy-start.1 = (f32[6144]{0:T(1024)S(1)}, f32[6144]{0:T(1024)}, u32[]{:S(2)}) copy-start(f32[6144]{0:T(1024)} %param.15) | copy-start | bytes 73732
Sparse Core Ops, SparseCore 0:
  10.1 152.4 all-gather.1
  390.5 56.8 reduce-scatter.1
